TPU v7x, 128 devices: a whole 4x4x4 slice. The times are simulated.
128 devices in a mesh: req: 8 (over x, core), seq: 16 (over z, y).
Axes of the slice: x: 4, y: 4, z: 4, core: 2. Of those that a mesh axis runs over, the one named last changes fastest.
Arguments:
- hidden: bfloat16 [8, 2048, 2048], P('req', 'seq'), may hold values from -6 to 6
- lengths: int32 [8], replicated, may hold values from 1 to 2048, 10240 in all
- slot_request: int32 [8], replicated, may hold values from 0 to 7, each once
- norm_gain: bfloat16 [2048], replicated, may hold values from 0.099609375 to 1.8984375
- in_weight: bfloat16 [2, 2048, 4096], P(None, 'req', 'seq'), may hold values from -0.125 to 0.125
- conv_weight: bfloat16 [4, 4096], P(None, 'seq'), may hold values from -3 to 3
- conv_bias: bfloat16 [4096], P('seq'), may hold values from -0.5 to 0.5
- xproj_weight: bfloat16 [4096, 160], P('seq'), may hold values from -0.09375 to 0.09375
- dt_weight: bfloat16 [128, 4096], P(None, 'seq'), may hold values from -0.5 to 0.5
- dt_bias: bfloat16 [4096], P('seq'), may hold values from -6.91 to -2.25
- a_log: float32 [16, 4096], replicated, may hold values from -2.3 to 1.39
- skip_gain: float32 [4096], replicated, may hold values from 0.5 to 1.5
- out_weight: bfloat16 [4096, 2048], P('seq', 'req'), may hold values from -0.09375 to 0.09375
Outputs:
- mixed: bfloat16 [8, 2048, 2048], P('req', 'seq')
- final_state: float32 [8, 16, 4096], P('req', None, 'seq')
Inputs may be any that keep to these rules, and one draw needn't show every extreme that they name: `lengths`: each slot's length is at least 1, the longest is exactly 2048, and they sum to 10240. `slot_request`: A permutation of the requests.
All inputs are finite; a program needn't handle non-finite values.
Results may differ from a plain program's by a relative error of at most 0.015.
Values may be sent and summed in bfloat16 or wider, within the bound.
No kernel may reach another device: no remote copies, remote signals or barrier semaphores. Data moves between devices by JAX's collectives and lax.ppermute only.
A program may use at most 128 MiB of HBM per device.

v0:
```python
import jax
import jax.numpy as jnp
from jax import lax
from jax.sharding import PartitionSpec as P

STATE = 16
RANK = 128


def shifted(block, axis, distance):
    devices = range(lax.axis_size(axis))
    route = [(i - distance, i) for i in devices if i - distance in devices]
    return lax.ppermute(block, axis, route)


def spread(array, axis, root):
    mine = lax.axis_index(axis) == root
    return lax.psum(jnp.where(mine, array, jnp.zeros_like(array)), axis)


def to_blocks(array):
    pieces, length, columns = array.shape
    return jnp.moveaxis(array.reshape(pieces, 16, length // 16, columns), 1, 0)


def from_blocks(array):
    count, pieces, group, columns = array.shape
    return jnp.moveaxis(array, 0, 1).reshape(pieces, count * group, columns)


def piece_scan(rates, values, entry, readout, decay):
    pieces, length, columns = rates.shape
    group = length // 16
    positions = jnp.arange(length, dtype=jnp.int32)
    lower = (positions[None, :] <= positions[:, None]).astype(jnp.float32)
    running = jnp.einsum("rs,psw->prw", lower, rates, precision=lax.Precision.HIGHEST)

    def advance(state, items):
        rate, value, into, outof = items
        outputs = []
        for place in range(group):
            factor = jnp.exp(rate[:, place][:, None, :] * decay[None])
            state = (
                factor * state
                + (rate[:, place] * value[:, place])[:, None, :] * into[:, place][:, :, None]
            )
            outputs.append(jnp.sum(outof[:, place][:, :, None] * state, axis=1))
        return (state, jnp.stack(outputs, axis=1))

    start = jnp.zeros((pieces, decay.shape[0], columns), jnp.float32)
    end_local, local_out = lax.scan(
        advance, start, (to_blocks(rates), to_blocks(values), to_blocks(entry), to_blocks(readout))
    )
    total_decay = jnp.exp(running[:, length - 1][:, None, :] * decay[None])
    return (end_local, from_blocks(local_out), total_decay, running)


def carried_part(running, readout, decay, carry_in):

    def correct(items):
        total, outof = items
        kept = jnp.exp(total[:, :, None, :] * decay[None, None]) * carry_in[:, None]
        return jnp.sum(outof[:, :, :, None] * kept, axis=2)

    return from_blocks(lax.map(correct, (to_blocks(running), to_blocks(readout))))


def per_device(
    hidden,
    lengths,
    slot_request,
    norm_gain,
    in_weight,
    conv_weight,
    conv_bias,
    xproj_weight,
    dt_weight,
    dt_bias,
    a_log,
    skip_gain,
    out_weight,
):
    seq_count = lax.axis_size("seq")
    seq_index = lax.axis_index("seq")
    req_index = lax.axis_index("req")
    rows = hidden.shape[1]
    span = rows * seq_count
    width = in_weight.shape[2]
    taps_count = conv_weight.shape[0]
    state_count = a_log.shape[0]
    total_inner = a_log.shape[1]
    tokens = hidden[0].astype(jnp.float32)
    scale = lax.rsqrt(jnp.mean(tokens * tokens, axis=-1, keepdims=True) + 1e-05)
    normed = (tokens * scale * norm_gain.astype(jnp.float32)).astype(jnp.bfloat16)
    w_in = lax.all_gather(in_weight, "req", axis=1, tiled=True)
    w_flat = jnp.concatenate((w_in[0], w_in[1]), axis=1)
    both = jnp.dot(
        lax.all_gather(normed, "seq", axis=0, tiled=True),
        w_flat,
        preferred_element_type=jnp.float32,
    )
    xin = both[:, :width]
    zgate = both[:, width:].astype(jnp.bfloat16)
    padded = jnp.pad(xin, ((taps_count - 1, 0), (0, 0)))
    taps = conv_weight.astype(jnp.float32)
    convolved = conv_bias.astype(jnp.float32) + jnp.zeros_like(xin)
    for tap in range(taps_count):
        convolved = convolved + taps[tap] * padded[tap : tap + span, :]
    inner = jax.nn.silu(convolved).astype(jnp.bfloat16)
    partial_proj = jnp.dot(inner, xproj_weight, preferred_element_type=jnp.float32)
    length_here = lax.dynamic_index_in_dim(lengths, req_index, 0, keepdims=False)
    summed = lax.psum(partial_proj, "seq")
    live_all = (jnp.arange(span, dtype=jnp.int32) < length_here).astype(jnp.float32)
    rate_low = summed[:, :RANK].astype(jnp.bfloat16)
    delta_ch = (
        jax.nn.softplus(
            jnp.dot(rate_low, dt_weight, preferred_element_type=jnp.float32)
            + dt_bias.astype(jnp.float32)
        )
        * live_all[:, None]
    )
    w_out = lax.all_gather(out_weight, "req", axis=1, tiled=True)
    inner_tok = lax.all_to_all(inner, "seq", split_axis=0, concat_axis=1, tiled=True)
    delta_tok = lax.all_to_all(
        delta_ch.astype(jnp.bfloat16), "seq", split_axis=0, concat_axis=1, tiled=True
    ).astype(delta_ch.dtype)
    own_proj = lax.dynamic_slice_in_dim(summed, seq_index * rows, rows, 0)
    decay = -jnp.exp(a_log)
    inner_f = inner_tok.astype(jnp.float32)
    entry = own_proj[None, :, RANK : RANK + STATE]
    readout = own_proj[None, :, RANK + STATE :]
    end_local, local_out, total_decay, running = piece_scan(
        delta_tok[None], inner_f[None], entry, readout, decay
    )
    zeros_state = jnp.zeros((state_count, total_inner), jnp.float32)

    def relay(turn, incoming):
        return shifted(total_decay[0] * incoming + end_local[0], "seq", 1)

    carry_in = lax.fori_loop(0, seq_count - 1, relay, zeros_state)
    carried = carried_part(running, readout, decay, carry_in[None])
    scanned = ((local_out + carried)[0] + skip_gain * inner_f).astype(jnp.bfloat16)
    last = spread(
        (total_decay[0] * carry_in + end_local[0]).astype(jnp.bfloat16), "seq", seq_count - 1
    ).astype(jnp.float32)
    mine = lax.dynamic_slice_in_dim(last, seq_index * width, width, 1)
    scanned_ch = lax.all_to_all(scanned, "seq", split_axis=1, concat_axis=0, tiled=True)
    gated_ch = (scanned_ch.astype(jnp.float32) * jax.nn.silu(zgate.astype(jnp.float32))).astype(
        jnp.bfloat16
    )
    branch = lax.psum_scatter(
        jnp.dot(gated_ch, w_out, preferred_element_type=jnp.float32).astype(jnp.bfloat16),
        "seq",
        scatter_dimension=0,
        tiled=True,
    ).astype(jnp.float32)
    slot_all = lax.all_gather(mine[None], "req", axis=0, tiled=True)
    picked = (slot_request == req_index).astype(jnp.float32)
    final_state = jnp.sum(picked[:, None, None] * slot_all, axis=0, keepdims=True)
    mixed = (tokens + branch).astype(jnp.bfloat16)[None]
    return (mixed, final_state)


def solution(mesh):
    in_specs = (
        P("req", "seq", None),
        P(),
        P(),
        P(),
        P(None, "req", "seq"),
        P(None, "seq"),
        P("seq"),
        P("seq", None),
        P(None, "seq"),
        P("seq"),
        P(),
        P(),
        P("seq", "req"),
    )
    out_specs = (P("req", "seq", None), P("req", None, "seq"))
    return jax.shard_map(
        per_device, mesh=mesh, in_specs=in_specs, out_specs=out_specs, check_vma=False
    )
```

profile of v0, /device:TPU:0, one launch (start us, length us, event | category | flops | bytes accessed | tf_op | source)
XLA Modules:
  0.0 717.7 jit_solution(14593859675135900258)
XLA Ops:
  12.1 25.4 %all-gather.7.cloned.1.call-done = bf16[2,2048,256]{2,1,0:T(8,128)(2,1)} async-done(((bf16[2,256,256]{2,1,0:T(8,128)(2,1)}), bf16[2,2048,256]{2,1,0:T(8,128)(2,1)}) %all-gather.7.cloned.1.call-update) | async-done | bytes 2097168 | tf_op jit(solution)/shard_map/all_gather | solution.py:95
  39.2 72.3 %all-gather.5.cloned.1.call-done = bf16[2048,2048]{1,0:T(8,128)(2,1)} async-done(((bf16[128,2048]{1,0:T(8,128)(2,1)}), bf16[2048,2048]{1,0:T(8,128)(2,1)}) %all-gather.5.cloned.1.call-update) | async-done | bytes 8388624 | tf_op jit(solution)/shard_map/all_gather | solution.py:98
  111.5 6.9 fusion.33
  122.7 2.8 fusion.56
  125.5 5.4 all-to-all-start.1
  132.2 88.7 %all-reduce.4.cloned.1.call-done = f32[2048,160]{0,1:T(8,128)} async-done(((f32[2048,160]{0,1:T(8,128)}), f32[2048,160]{0,1:T(8,128)}) %all-reduce.4.cloned.1.call-update) | async-done | bytes 1310736 | tf_op jit(solution)/shard_map/psum | solution.py:112
  220.9 2.7 fusion.32
  225.0 5.1 all-to-all-start
  234.1 2.8 reshape.994
  238.4 7.5 %all-to-all-done = bf16[16,128,256]{1,2,0:T(8,128)(2,1)S(1)} async-done(((bf16[16,128,256]{1,2,0:T(8,128)(2,1)}), bf16[16,128,256]{1,2,0:T(8,128)(2,1)S(1)}, u32[]{:S(2)}, u32[]{:S(2)}) %all-to-all-start) | async-done | bytes 1048608 | tf_op jit(solution)/shard_map/all_to_all | solution.py:124
  255.7 65.7 %while.35 = (s32[]{:T(128)}, f32[1,16,4096]{2,1,0:T(8,128)S(1)}, f32[16,1,8,4096]{3,2,1,0:T(8,128)}, f32[16,1,8,4096]{3,2,1,0:T(8,128)}, f32[16,4096]{1,0:T(8,12...) while((s32[]{:T(128)}, f32[1,16,4096]{2,1,0:T(8,128)S(1)}, ...), condition=%wide.region_11.12_spmd.clone, body=%wide.region_2.11_spmd.clone.sunk | while | flops 4849667 | bytes 4347896 | solution.py:51
  321.5 148.6 %while.33 = (s32[]{:T(128)}, f32[16,4096]{1,0:T(8,128)S(1)}, f32[1,16,4096]{2,1,0:T(8,128)S(1)}, f32[1,16,4096]{2,1,0:T(8,128)S(1)}, s32[]{:T(128)}) while((s32[]{:T(128)}, f32[16,4096]{1,0:T(8,128)S(1)}, f32[1,16,4096]{2,1,0:T(8,128)S(1)}, f32[1,16,4096]{2,1,0:T(8,128)S(1)}, s32[]{:T(128)}) %tuple.124), condition=%wide.region_13.14_spmd, body=%wide.region_12.13_spmd.sunk | while | flops 131074 | bytes 2097253 | solution.py:140
  324.1 3.9 collective-permute-done
  328.0 4.4 collective-permute-start
  332.4 5.0 collective-permute-done
  337.4 4.4 collective-permute-start
  341.8 6.1 collective-permute-done
  347.9 4.4 collective-permute-start
  352.4 6.1 collective-permute-done
  358.5 4.4 collective-permute-start
  362.9 5.2 collective-permute-done
  368.1 4.4 collective-permute-start
  372.5 4.3 collective-permute-done
  376.9 4.4 collective-permute-start
  381.3 3.9 collective-permute-done
  385.2 6.8 collective-permute-start
  392.1 5.6 collective-permute-done
  397.7 6.2 collective-permute-start
  404.0 4.5 collective-permute-done
  408.5 5.6 collective-permute-start
  414.1 3.9 collective-permute-done
  418.0 6.5 collective-permute-start
  424.5 3.9 collective-permute-done
  428.4 6.5 collective-permute-start
  435.0 3.9 collective-permute-done
  438.9 6.5 collective-permute-start
  445.4 3.9 collective-permute-done
  449.3 6.5 collective-permute-start
  455.8 3.9 collective-permute-done
  459.7 6.5 collective-permute-start
  466.2 3.9 collective-permute-done
  471.6 35.8 %while.34 = (s32[]{:T(128)}, f32[16,1,8,4096]{3,2,1,0:T(8,128)}, f32[16,1,8,16]{3,2,1,0:T(8,128)S(1)}, f32[16,1,8,4096]{3,2,1,0:T(8,128)}, f32[16,4096]{1,0:T(8,128)S(1)}, /*index=5*/f32[16,4096]{1,0:T(8,128)S(1)}, s32[]{:T(128)}) while((s32[]{:T(128)}, f32[16,1,8,4096]{3,2,1,0:T(8,128)}, f32[16,1,8,16]{3,2,1,0:T(8,128)S(1)}, ...), condition=%wide.region_16.17_spmd, body=%wide.region_14.16_spmd.sunk | while | flops 2064386 | bytes 1312853 | solution.py:65
  512.9 18.0 %all-to-all-start.2 = ((bf16[128,16,256]{2,0,1:T(8,128)(2,1)}), bf16[128,16,256]{2,0,1:T(8,128)(2,1)S(1)}, u32[]{:S(2)}, u32[]{:S(2)}) async-start(bf16[128,16,256]{2,0,1:T(8,128)(2,1)} %fusion.30), calls=%async_computation.2 | async-start | bytes 2097152 | tf_op jit(solution)/shard_map/all_to_all | solution.py:147
  532.1 12.2 %all-to-all-done.2 = bf16[128,16,256]{2,0,1:T(8,128)(2,1)S(1)} async-done(((bf16[128,16,256]{2,0,1:T(8,128)(2,1)}), bf16[128,16,256]{2,0,1:T(8,128)(2,1)S(1)}, u32[]{:S(2)}, u32[]{:S(2)}) %all-to-all-start.2) | async-done | bytes 1048608 | tf_op jit(solution)/shard_map/all_to_all | solution.py:147
  546.7 6.8 convolution_convert_fusion
  554.1 66.1 %all-reduce.6.cloned.1.call-done = bf16[16,4096]{1,0:T(8,128)(2,1)} async-done(((bf16[16,4096]{1,0:T(8,128)(2,1)}), bf16[16,4096]{1,0:T(8,128)(2,1)}) %all-reduce.6.cloned.1.call-update) | async-done | bytes 131088 | tf_op jit(solution)/shard_map/psum | solution.py:18
  620.9 13.0 %all-gather = f32[128,256]{1,0:T(8,128)S(1)} all-gather(f32[16,256]{1,0:T(8,128)S(1)} %dynamic-slice_convert_fusion), channel_id=2, replica_groups=mesh['req'=8,'seq'=16] {'req'}, dimensions={0}, use_global_device_ids=true | all-gather | bytes 147456 | tf_op jit(solution)/shard_map/all_gather | solution.py:157
  634.6 74.3 %reduce-scatter.2.cloned.1.call-done = bf16[128,2048]{1,0:T(8,128)(2,1)} async-done(((bf16[2048,2048]{1,0:T(8,128)(2,1)}), bf16[128,2048]{1,0:T(8,128)(2,1)}) %reduce-scatter.2.cloned.1.call-update) | async-done | bytes 524304 | tf_op jit(solution)/shard_map/reduce_scatter | solution.py:151
  (340 shorter events, 146.6 us)
Async XLA Ops:
  7.2 115.5 %copy-start = (bf16[256,160]{0,1:T(8,128)(2,1)S(1)}, bf16[256,160]{0,1:T(8,128)(2,1)}, u32[]{:S(2)}) copy-start(bf16[256,160]{0,1:T(8,128)(2,1)} %param.26) | copy-start | bytes 245764
  7.2 4.8 copy-start.12
  7.2 4.8 copy-start.10
  7.2 30.3 %all-gather.7.cloned.1.call-start = ((), (), s32[]{:S(2)}) async-start(), calls=%async_computation.5 | async-start | bytes 2359296 | tf_op jit(solution)/shard_map/all_gather | solution.py:95
  7.9 103.6 %all-gather.5.cloned.1.call-start = ((), (), s32[]{:S(2)}) async-start(), calls=%async_computation.4 | async-start | bytes 8912896 | tf_op jit(solution)/shard_map/all_gather | solution.py:98
  12.0 209.0 %all-reduce.4.cloned.1.call-start = ((), (), s32[]{:S(2)}) async-start(), calls=%async_computation.6 | async-start | bytes 2621440 | tf_op jit(solution)/shard_map/psum | solution.py:112
  118.4 2.0 copy-start.4
  125.5 5.5 copy-start.13
  125.5 5.5 copy-start.14
  125.5 95.4 %copy-start.11 = (bf16[128,256]{1,0:T(8,128)(2,1)S(1)}, bf16[128,256]{1,0:T(8,128)(2,1)}, u32[]{:S(2)}) copy-start(bf16[128,256]{1,0:T(8,128)(2,1)} %param.27) | copy-start | bytes 196612
  125.5 99.5 %all-to-all-start.1 = ((bf16[16,128,256]{2,1,0:T(8,128)(2,1)}), bf16[16,128,256]{2,1,0:T(8,128)(2,1)S(1)}, u32[]{:S(2)}, u32[]{:S(2)}) async-start(bf16[16,128,256]{2,1,0:T(8,128)(2,1)} %bitcast.17), calls=%async_computation.1 | async-start | bytes 2097152 | tf_op jit(solution)/shard_map/all_to_all | solution.py:123
  223.6 7.1 copy-start.9
  225.0 20.9 %all-to-all-start = ((bf16[16,128,256]{1,2,0:T(8,128)(2,1)}), bf16[16,128,256]{1,2,0:T(8,128)(2,1)S(1)}, u32[]{:S(2)}, u32[]{:S(2)}) async-start(bf16[16,128,256]{1,2,0:T(8,128)(2,1)} %copy.43), calls=%async_computation | async-start | bytes 2097152 | tf_op jit(solution)/shard_map/all_to_all | solution.py:124
  230.1 316.6 %all-gather.9.cloned.1.call-start = ((), (), s32[]{:S(2)}) async-start(), calls=%async_computation.7 | async-start | bytes 1179648 | tf_op jit(solution)/shard_map/all_gather | solution.py:122
  246.3 1.3 copy-start.3
  247.7 5.4 copy-start.6
  321.5 6.4 collective-permute-start
  328.0 9.4 %collective-permute-start = (f32[16,4096]{1,0:T(8,128)S(1)}, f32[16,4096]{1,0:T(8,128)S(1)}, u32[]{:S(2)}, u32[]{:S(2)}) collective-permute-start(f32[16,4096]{1,0:T(8,128)S(1)} %bitcast_add_fusion.3), channel_id=1, source_target_pairs={{0,1},{1,2},{2,3},{3,4},{4,5},{5,6},{6,7},{7,8},{8,9},{9,10},{10,1... | collective-permute-start | bytes 786440 | tf_op jit(solution)/shard_map/while/body/eval_jaxpr/ppermute | solution.py:13
  337.4 10.5 %collective-permute-start = (f32[16,4096]{1,0:T(8,128)S(1)}, f32[16,4096]{1,0:T(8,128)S(1)}, u32[]{:S(2)}, u32[]{:S(2)}) collective-permute-start(f32[16,4096]{1,0:T(8,128)S(1)} %bitcast_add_fusion.3), channel_id=1, source_target_pairs={{0,1},{1,2},{2,3},{3,4},{4,5},{5,6},{6,7},{7,8},{8,9},{9,10},{10,1... | collective-permute-start | bytes 786440 | tf_op jit(solution)/shard_map/while/body/eval_jaxpr/ppermute | solution.py:13
  347.9 10.5 %collective-permute-start = (f32[16,4096]{1,0:T(8,128)S(1)}, f32[16,4096]{1,0:T(8,128)S(1)}, u32[]{:S(2)}, u32[]{:S(2)}) collective-permute-start(f32[16,4096]{1,0:T(8,128)S(1)} %bitcast_add_fusion.3), channel_id=1, source_target_pairs={{0,1},{1,2},{2,3},{3,4},{4,5},{5,6},{6,7},{7,8},{8,9},{9,10},{10,1... | collective-permute-start | bytes 786440 | tf_op jit(solution)/shard_map/while/body/eval_jaxpr/ppermute | solution.py:13
  358.5 9.6 %collective-permute-start = (f32[16,4096]{1,0:T(8,128)S(1)}, f32[16,4096]{1,0:T(8,128)S(1)}, u32[]{:S(2)}, u32[]{:S(2)}) collective-permute-start(f32[16,4096]{1,0:T(8,128)S(1)} %bitcast_add_fusion.3), channel_id=1, source_target_pairs={{0,1},{1,2},{2,3},{3,4},{4,5},{5,6},{6,7},{7,8},{8,9},{9,10},{10,1... | collective-permute-start | bytes 786440 | tf_op jit(solution)/shard_map/while/body/eval_jaxpr/ppermute | solution.py:13
  368.1 8.8 %collective-permute-start = (f32[16,4096]{1,0:T(8,128)S(1)}, f32[16,4096]{1,0:T(8,128)S(1)}, u32[]{:S(2)}, u32[]{:S(2)}) collective-permute-start(f32[16,4096]{1,0:T(8,128)S(1)} %bitcast_add_fusion.3), channel_id=1, source_target_pairs={{0,1},{1,2},{2,3},{3,4},{4,5},{5,6},{6,7},{7,8},{8,9},{9,10},{10,1... | collective-permute-start | bytes 786440 | tf_op jit(solution)/shard_map/while/body/eval_jaxpr/ppermute | solution.py:13
  376.9 8.3 %collective-permute-start = (f32[16,4096]{1,0:T(8,128)S(1)}, f32[16,4096]{1,0:T(8,128)S(1)}, u32[]{:S(2)}, u32[]{:S(2)}) collective-permute-start(f32[16,4096]{1,0:T(8,128)S(1)} %bitcast_add_fusion.3), channel_id=1, source_target_pairs={{0,1},{1,2},{2,3},{3,4},{4,5},{5,6},{6,7},{7,8},{8,9},{9,10},{10,1... | collective-permute-start | bytes 786440 | tf_op jit(solution)/shard_map/while/body/eval_jaxpr/ppermute | solution.py:13
  385.2 12.5 %collective-permute-start = (f32[16,4096]{1,0:T(8,128)S(1)}, f32[16,4096]{1,0:T(8,128)S(1)}, u32[]{:S(2)}, u32[]{:S(2)}) collective-permute-start(f32[16,4096]{1,0:T(8,128)S(1)} %bitcast_add_fusion.3), channel_id=1, source_target_pairs={{0,1},{1,2},{2,3},{3,4},{4,5},{5,6},{6,7},{7,8},{8,9},{9,10},{10,1... | collective-permute-start | bytes 786440 | tf_op jit(solution)/shard_map/while/body/eval_jaxpr/ppermute | solution.py:13
  397.7 10.7 %collective-permute-start = (f32[16,4096]{1,0:T(8,128)S(1)}, f32[16,4096]{1,0:T(8,128)S(1)}, u32[]{:S(2)}, u32[]{:S(2)}) collective-permute-start(f32[16,4096]{1,0:T(8,128)S(1)} %bitcast_add_fusion.3), channel_id=1, source_target_pairs={{0,1},{1,2},{2,3},{3,4},{4,5},{5,6},{6,7},{7,8},{8,9},{9,10},{10,1... | collective-permute-start | bytes 786440 | tf_op jit(solution)/shard_map/while/body/eval_jaxpr/ppermute | solution.py:13
  408.5 9.5 %collective-permute-start = (f32[16,4096]{1,0:T(8,128)S(1)}, f32[16,4096]{1,0:T(8,128)S(1)}, u32[]{:S(2)}, u32[]{:S(2)}) collective-permute-start(f32[16,4096]{1,0:T(8,128)S(1)} %bitcast_add_fusion.3), channel_id=1, source_target_pairs={{0,1},{1,2},{2,3},{3,4},{4,5},{5,6},{6,7},{7,8},{8,9},{9,10},{10,1... | collective-permute-start | bytes 786440 | tf_op jit(solution)/shard_map/while/body/eval_jaxpr/ppermute | solution.py:13
  418.0 10.4 %collective-permute-start = (f32[16,4096]{1,0:T(8,128)S(1)}, f32[16,4096]{1,0:T(8,128)S(1)}, u32[]{:S(2)}, u32[]{:S(2)}) collective-permute-start(f32[16,4096]{1,0:T(8,128)S(1)} %bitcast_add_fusion.3), channel_id=1, source_target_pairs={{0,1},{1,2},{2,3},{3,4},{4,5},{5,6},{6,7},{7,8},{8,9},{9,10},{10,1... | collective-permute-start | bytes 786440 | tf_op jit(solution)/shard_map/while/body/eval_jaxpr/ppermute | solution.py:13
  428.4 10.4 %collective-permute-start = (f32[16,4096]{1,0:T(8,128)S(1)}, f32[16,4096]{1,0:T(8,128)S(1)}, u32[]{:S(2)}, u32[]{:S(2)}) collective-permute-start(f32[16,4096]{1,0:T(8,128)S(1)} %bitcast_add_fusion.3), channel_id=1, source_target_pairs={{0,1},{1,2},{2,3},{3,4},{4,5},{5,6},{6,7},{7,8},{8,9},{9,10},{10,1... | collective-permute-start | bytes 786440 | tf_op jit(solution)/shard_map/while/body/eval_jaxpr/ppermute | solution.py:13
  438.9 10.4 %collective-permute-start = (f32[16,4096]{1,0:T(8,128)S(1)}, f32[16,4096]{1,0:T(8,128)S(1)}, u32[]{:S(2)}, u32[]{:S(2)}) collective-permute-start(f32[16,4096]{1,0:T(8,128)S(1)} %bitcast_add_fusion.3), channel_id=1, source_target_pairs={{0,1},{1,2},{2,3},{3,4},{4,5},{5,6},{6,7},{7,8},{8,9},{9,10},{10,1... | collective-permute-start | bytes 786440 | tf_op jit(solution)/shard_map/while/body/eval_jaxpr/ppermute | solution.py:13
  449.3 10.4 %collective-permute-start = (f32[16,4096]{1,0:T(8,128)S(1)}, f32[16,4096]{1,0:T(8,128)S(1)}, u32[]{:S(2)}, u32[]{:S(2)}) collective-permute-start(f32[16,4096]{1,0:T(8,128)S(1)} %bitcast_add_fusion.3), channel_id=1, source_target_pairs={{0,1},{1,2},{2,3},{3,4},{4,5},{5,6},{6,7},{7,8},{8,9},{9,10},{10,1... | collective-permute-start | bytes 786440 | tf_op jit(solution)/shard_map/while/body/eval_jaxpr/ppermute | solution.py:13
  459.7 10.4 %collective-permute-start = (f32[16,4096]{1,0:T(8,128)S(1)}, f32[16,4096]{1,0:T(8,128)S(1)}, u32[]{:S(2)}, u32[]{:S(2)}) collective-permute-start(f32[16,4096]{1,0:T(8,128)S(1)} %bitcast_add_fusion.3), channel_id=1, source_target_pairs={{0,1},{1,2},{2,3},{3,4},{4,5},{5,6},{6,7},{7,8},{8,9},{9,10},{10,1... | collective-permute-start | bytes 786440 | tf_op jit(solution)/shard_map/while/body/eval_jaxpr/ppermute | solution.py:13
  509.9 0.7 copy-start.8
  512.9 18.1 %copy-start.5 = (f32[16,4096]{1,0:T(8,128)S(1)}, f32[16,4096]{1,0:T(8,128)}, u32[]{:S(2)}) copy-start(f32[16,4096]{1,0:T(8,128)} %param.29) | copy-start | bytes 786436
  512.9 18.1 %copy-start.7 = (f32[1,1,4096]{2,1,0:T(1,128)S(1)}, f32[1,1,4096]{2,1,0:T(1,128)}, u32[]{:S(2)}) copy-start(f32[1,1,4096]{2,1,0:T(1,128)} %copy-done.6) | copy-start | bytes 49156
  512.9 31.4 %all-to-all-start.2 = ((bf16[128,16,256]{2,0,1:T(8,128)(2,1)}), bf16[128,16,256]{2,0,1:T(8,128)(2,1)S(1)}, u32[]{:S(2)}, u32[]{:S(2)}) async-start(bf16[128,16,256]{2,0,1:T(8,128)(2,1)} %fusion.30), calls=%async_computation.2 | async-start | bytes 2097152 | tf_op jit(solution)/shard_map/all_to_all | solution.py:147
  531.0 89.2 %all-reduce.6.cloned.1.call-start = ((), (), s32[]{:S(2)}) async-start(), calls=%async_computation.9 | async-start | bytes 262144 | tf_op jit(solution)/shard_map/psum | solution.py:18
  531.8 177.1 %reduce-scatter.2.cloned.1.call-start = ((), (), s32[]{:S(2)}) async-start(), calls=%async_computation.8 | async-start | bytes 8912896 | tf_op jit(solution)/shard_map/reduce_scatter | solution.py:151
  553.5 0.7 copy-start.15
  553.5 155.5 %copy-start.2 = (bf16[1,128,2048]{2,1,0:T(8,128)(2,1)S(1)}, bf16[1,128,2048]{2,1,0:T(8,128)(2,1)}, u32[]{:S(2)}) copy-start(bf16[1,128,2048]{2,1,0:T(8,128)(2,1)} %param.19) | copy-start | bytes 1572868
  553.5 157.4 %copy-start.1 = (bf16[256,160]{0,1:T(8,128)(2,1)S(1)}, bf16[256,160]{0,1:T(8,128)(2,1)}, u32[]{:S(2)}) copy-start(bf16[256,160]{0,1:T(8,128)(2,1)} %param.26) | copy-start | bytes 245764
Sparse Core Ops, SparseCore 0:
  9.7 27.7 all-gather.6
  40.2 71.2 all-gather.4
  125.6 95.2 all-reduce.3
  232.3 24.7 all-gather.8
  535.2 84.9 all-reduce.5
  623.5 85.3 reduce-scatter.1
where the time goes:
time: 720 us; the launch traced here: 718 us
  waiting for transfers between devices  415 us (58%)
  starting transfers between devices  109 us (15%)
  local copies, waits for them, and re-layouts  89.9 us (12%)
  other arithmetic  54.7 us (8%)
  matrix products  19.6 us (3%)
  between operations  14.4 us (2%)
  blocking collectives  13 us (2%)
    psum x1, waiting for transfers between devices, per_device(): summed = lax.psum(partial_proj, 'seq')  88.7 us
    ppermute x15, starting transfers between devices, shifted(): return lax.ppermute(block, axis, route)  80.1 us
    reduce_scatter x1, waiting for transfers between devices, per_device(): lax.psum_scatter(jnp.dot(gated_ch, w_out, preferred_element_type=jnp.floa...  74.3 us
    all_gather x1, waiting for transfers between devices, per_device(): lax.all_gather(normed, 'seq', axis=0, tiled=True)  72.3 us
    ppermute x15, waiting for transfers between devices, shifted(): return lax.ppermute(block, axis, route)  67.6 us
    psum x1, waiting for transfers between devices, spread(): return lax.psum(jnp.where(mine, array, jnp.zeros_like(array)), axis)  66.1 us
    squeeze x32, local copies, waits for them, and re-layouts, piece_scan(): lax.scan(advance, start, (to_blocks(rates), to_blocks(values), to_blocks(...  26.9 us
    all_gather x1, waiting for transfers between devices, per_device(): w_in = lax.all_gather(in_weight, 'req', axis=1, tiled=True)  25.4 us
  transfers between devices with their start and end apart: 24, of which 22 were waited for; matrix products, arithmetic and copies ran while one was open for 20% of the time, Pallas kernels for 0%

commit v1 on v0

--- a/solution.py
+++ b/solution.py
@@ -109,7 +109,9 @@
     inner = jax.nn.silu(convolved).astype(jnp.bfloat16)
     partial_proj = jnp.dot(inner, xproj_weight, preferred_element_type=jnp.float32)
     length_here = lax.dynamic_index_in_dim(lengths, req_index, 0, keepdims=False)
-    summed = lax.psum(partial_proj, "seq")
+    summed = partial_proj
+    for hop in (1, 2, 4, 8):
+        summed = summed + lax.ppermute(summed, "seq", [(dev, dev ^ hop) for dev in range(16)])
     live_all = (jnp.arange(span, dtype=jnp.int32) < length_here).astype(jnp.float32)
     rate_low = summed[:, :RANK].astype(jnp.bfloat16)
     delta_ch = (

time: 720 us -> 748 us (1.039)
  waiting for transfers between devices: 415 us -> 443 us
  starting transfers between devices: 109 us -> 121 us
  local copies, waits for them, and re-layouts: 89.9 us -> 80 us
    ppermute x0 -> x4, waiting for transfers between devices: none -> 115 us  [per_device(): lax.ppermute(summed, 'seq', [(dev, dev ^ hop) for dev in range(16)])]
    psum x1 -> x0, waiting for transfers between devices: 88.7 us -> none  [per_device(): summed = lax.psum(partial_proj, 'seq')]
    squeeze x32, local copies, waits for them, and re-layouts: 26.9 us -> 15.9 us  [piece_scan(): lax.scan(advance, start, (to_blocks(rates), to_blocks(values), to_blocks(...]
    ppermute x0 -> x4, starting transfers between devices: none -> 9.09 us  [per_device(): lax.ppermute(summed, 'seq', [(dev, dev ^ hop) for dev in range(16)])]
  transfers between devices with their start and end apart: 24 -> 27, of which waited for: 22 -> 25; matrix products, arithmetic and copies ran while one was open for 20% -> 18% of each run, Pallas kernels for 0% -> 0%
where the time goes in v1:
time: 748 us; the launch traced here: 746 us
  waiting for transfers between devices  443 us (59%)
  starting transfers between devices  121 us (16%)
  local copies, waits for them, and re-layouts  80 us (11%)
  other arithmetic  55.7 us (7%)
  matrix products  17.3 us (2%)
  between operations  14.1 us (2%)
  blocking collectives  13 us (2%)
    ppermute x4, waiting for transfers between devices, per_device(): lax.ppermute(summed, 'seq', [(dev, dev ^ hop) for dev in range(16)])  115 us
    ppermute x15, starting transfers between devices, shifted(): return lax.ppermute(block, axis, route)  84.6 us
    reduce_scatter x1, waiting for transfers between devices, per_device(): lax.psum_scatter(jnp.dot(gated_ch, w_out, preferred_element_type=jnp.floa...  74.4 us
    all_gather x1, waiting for transfers between devices, per_device(): lax.all_gather(normed, 'seq', axis=0, tiled=True)  72.3 us
    ppermute x15, waiting for transfers between devices, shifted(): return lax.ppermute(block, axis, route)  69.6 us
    psum x1, waiting for transfers between devices, spread(): return lax.psum(jnp.where(mine, array, jnp.zeros_like(array)), axis)  65.8 us
    all_gather x1, waiting for transfers between devices, per_device(): w_in = lax.all_gather(in_weight, 'req', axis=1, tiled=True)  25.5 us
    dynamic_update_slice x32, local copies, waits for them, and re-layouts, piece_scan(): lax.scan(advance, start, (to_blocks(rates), to_blocks(values), to_blocks(...  21.3 us
  transfers between devices with their start and end apart: 27, of which 25 were waited for; matrix products, arithmetic and copies ran while one was open for 18% of the time, Pallas kernels for 0%

profile of v1, /device:TPU:0, one launch (start us, length us, event | category | flops | bytes accessed | tf_op | source)
XLA Modules:
  0.0 746.0 jit_solution(4297703062251797324)
XLA Ops:
  12.0 25.5 %all-gather.7.cloned.1.call-done = bf16[2,2048,256]{2,1,0:T(8,128)(2,1)} async-done(((bf16[2,256,256]{2,1,0:T(8,128)(2,1)}), bf16[2,2048,256]{2,1,0:T(8,128)(2,1)}) %all-gather.7.cloned.1.call-update) | async-done | bytes 2097168 | tf_op jit(solution)/shard_map/all_gather | solution.py:95
  39.2 72.3 %all-gather.5.cloned.1.call-done = bf16[2048,2048]{1,0:T(8,128)(2,1)} async-done(((bf16[128,2048]{1,0:T(8,128)(2,1)}), bf16[2048,2048]{1,0:T(8,128)(2,1)}) %all-gather.5.cloned.1.call-update) | async-done | bytes 8388624 | tf_op jit(solution)/shard_map/all_gather | solution.py:98
  111.5 6.9 fusion.33
  126.0 28.9 %collective-permute-done.1 = f32[2048,160]{0,1:T(8,128)S(1)} collective-permute-done((f32[2048,160]{0,1:T(8,128)S(1)}, f32[2048,160]{0,1:T(8,128)S(1)}, u32[]{:S(2)}, u32[]{:S(2)}) %collective-permute-start.1) | collective-permute-done | bytes 1310752 | tf_op jit(solution)/shard_map/ppermute | solution.py:114
  158.1 28.0 %collective-permute-done.2 = f32[2048,160]{0,1:T(8,128)S(1)} collective-permute-done((f32[2048,160]{0,1:T(8,128)S(1)}, f32[2048,160]{0,1:T(8,128)S(1)}, u32[]{:S(2)}, u32[]{:S(2)}) %collective-permute-start.2) | collective-permute-done | bytes 1310752 | tf_op jit(solution)/shard_map/ppermute | solution.py:114
  187.7 27.3 %collective-permute-done.3 = f32[2048,160]{0,1:T(8,128)S(1)} collective-permute-done((f32[2048,160]{0,1:T(8,128)S(1)}, f32[2048,160]{0,1:T(8,128)S(1)}, u32[]{:S(2)}, u32[]{:S(2)}) %collective-permute-start.3) | collective-permute-done | bytes 1310752 | tf_op jit(solution)/shard_map/ppermute | solution.py:114
  218.2 4.6 all-to-all-start.1
  224.1 31.2 %collective-permute-done.4 = f32[2048,160]{0,1:T(8,128)} collective-permute-done((f32[2048,160]{0,1:T(8,128)S(1)}, f32[2048,160]{0,1:T(8,128)}, u32[]{:S(2)}, u32[]{:S(2)}) %collective-permute-start.4) | collective-permute-done | bytes 1310752 | tf_op jit(solution)/shard_map/ppermute | solution.py:114
  259.6 5.4 all-to-all-start
  272.2 6.5 all-to-all-done
  289.7 55.2 %while.35 = (s32[]{:T(128)}, f32[1,16,4096]{2,1,0:T(8,128)S(1)}, f32[16,1,8,4096]{3,2,1,0:T(8,128)}, f32[16,1,8,4096]{3,2,1,0:T(8,128)}, f32[16,4096]{1,0:T(8,12...) while((s32[]{:T(128)}, f32[1,16,4096]{2,1,0:T(8,128)S(1)}, ...), condition=%wide.region_10.11_spmd.clone, body=%wide.region_1.10_spmd.clone.sunk | while | flops 4849667 | bytes 4347896 | solution.py:51
  344.9 155.0 %while.33 = (s32[]{:T(128)}, f32[16,4096]{1,0:T(8,128)S(1)}, f32[1,16,4096]{2,1,0:T(8,128)S(1)}, f32[1,16,4096]{2,1,0:T(8,128)S(1)}, s32[]{:T(128)}) while((s32[]{:T(128)}, f32[16,4096]{1,0:T(8,128)S(1)}, f32[1,16,4096]{2,1,0:T(8,128)S(1)}, f32[1,16,4096]{2,1,0:T(8,128)S(1)}, s32[]{:T(128)}) %tuple.124), condition=%wide.region_12.13_spmd, body=%wide.region_11.12_spmd.sunk | while | flops 131074 | bytes 2097253 | solution.py:142
  347.4 5.9 collective-permute-done
  353.4 4.4 collective-permute-start
  357.8 6.2 collective-permute-done
  364.1 4.4 collective-permute-start
  368.5 5.4 collective-permute-done
  373.9 4.4 collective-permute-start
  378.3 4.5 collective-permute-done
  382.9 4.4 collective-permute-start
  387.3 3.9 collective-permute-done
  391.2 5.1 collective-permute-start
  396.4 4.8 collective-permute-done
  401.2 5.6 collective-permute-start
  406.9 3.9 collective-permute-done
  410.8 6.5 collective-permute-start
  417.3 3.9 collective-permute-done
  421.2 6.5 collective-permute-start
  427.7 3.9 collective-permute-done
  431.6 6.5 collective-permute-start
  438.1 3.9 collective-permute-done
  442.0 6.5 collective-permute-start
  448.5 4.1 collective-permute-done
  452.7 6.8 collective-permute-start
  459.5 5.2 collective-permute-done
  464.8 7.1 collective-permute-start
  471.9 6.4 collective-permute-done
  478.3 7.4 collective-permute-start
  485.7 3.9 collective-permute-done
  489.6 6.5 collective-permute-start
  496.1 3.9 collective-permute-done
  501.5 35.9 %while.34 = (s32[]{:T(128)}, f32[16,1,8,4096]{3,2,1,0:T(8,128)}, f32[16,1,8,16]{3,2,1,0:T(8,128)S(1)}, f32[16,1,8,4096]{3,2,1,0:T(8,128)}, f32[16,4096]{1,0:T(8,128)S(1)}, /*index=5*/f32[16,4096]{1,0:T(8,128)S(1)}, s32[]{:T(128)}) while((s32[]{:T(128)}, f32[16,1,8,4096]{3,2,1,0:T(8,128)}, f32[16,1,8,16]{3,2,1,0:T(8,128)S(1)}, ...), condition=%wide.region_15.16_spmd, body=%wide.region_13.15_spmd.sunk | while | flops 2064386 | bytes 1312853 | solution.py:65
  542.8 16.9 %all-to-all-start.2 = ((bf16[128,16,256]{2,0,1:T(8,128)(2,1)}), bf16[128,16,256]{2,0,1:T(8,128)(2,1)S(1)}, u32[]{:S(2)}, u32[]{:S(2)}) async-start(bf16[128,16,256]{2,0,1:T(8,128)(2,1)} %fusion.30), calls=%async_computation.2 | async-start | bytes 2097152 | tf_op jit(solution)/shard_map/all_to_all | solution.py:149
  560.9 12.2 %all-to-all-done.2 = bf16[128,16,256]{2,0,1:T(8,128)(2,1)S(1)} async-done(((bf16[128,16,256]{2,0,1:T(8,128)(2,1)}), bf16[128,16,256]{2,0,1:T(8,128)(2,1)S(1)}, u32[]{:S(2)}, u32[]{:S(2)}) %all-to-all-start.2) | async-done | bytes 1048608 | tf_op jit(solution)/shard_map/all_to_all | solution.py:149
  575.5 6.8 convolution_convert_fusion
  582.9 65.8 %all-reduce.3.cloned.1.call-done = bf16[16,4096]{1,0:T(8,128)(2,1)} async-done(((bf16[16,4096]{1,0:T(8,128)(2,1)}), bf16[16,4096]{1,0:T(8,128)(2,1)}) %all-reduce.3.cloned.1.call-update) | async-done | bytes 131088 | tf_op jit(solution)/shard_map/psum | solution.py:18
  649.5 13.0 %all-gather = f32[128,256]{1,0:T(8,128)S(1)} all-gather(f32[16,256]{1,0:T(8,128)S(1)} %dynamic-slice_convert_fusion), channel_id=2, replica_groups=mesh['req'=8,'seq'=16] {'req'}, dimensions={0}, use_global_device_ids=true | all-gather | bytes 147456 | tf_op jit(solution)/shard_map/all_gather | solution.py:159
  663.2 74.4 %reduce-scatter.2.cloned.1.call-done = bf16[128,2048]{1,0:T(8,128)(2,1)} async-done(((bf16[2048,2048]{1,0:T(8,128)(2,1)}), bf16[128,2048]{1,0:T(8,128)(2,1)}) %reduce-scatter.2.cloned.1.call-update) | async-done | bytes 524304 | tf_op jit(solution)/shard_map/reduce_scatter | solution.py:153
  (345 shorter events, 152.7 us)
Async XLA Ops:
  7.2 115.5 %copy-start = (bf16[256,160]{0,1:T(8,128)(2,1)S(1)}, bf16[256,160]{0,1:T(8,128)(2,1)}, u32[]{:S(2)}) copy-start(bf16[256,160]{0,1:T(8,128)(2,1)} %param.26) | copy-start | bytes 245764
  7.2 4.8 copy-start.10
  7.2 4.8 copy-start.8
  7.2 30.3 %all-gather.7.cloned.1.call-start = ((), (), s32[]{:S(2)}) async-start(), calls=%async_computation.5 | async-start | bytes 2359296 | tf_op jit(solution)/shard_map/all_gather | solution.py:95
  7.9 103.6 %all-gather.5.cloned.1.call-start = ((), (), s32[]{:S(2)}) async-start(), calls=%async_computation.4 | async-start | bytes 8912896 | tf_op jit(solution)/shard_map/all_gather | solution.py:98
  118.4 2.0 copy-start.4
  124.4 30.4 %collective-permute-start.1 = (f32[2048,160]{0,1:T(8,128)S(1)}, f32[2048,160]{0,1:T(8,128)S(1)}, u32[]{:S(2)}, u32[]{:S(2)}) collective-permute-start(f32[2048,160]{0,1:T(8,128)S(1)} %fusion.56), channel_id=1, source_target_pairs={{0,1},{1,0},{2,3},{3,2},{4,5},{5,4},{6,7},{7,6},{8,9},{9,8},{10,11... | collective-permute-start | bytes 3932168 | tf_op jit(solution)/shard_map/ppermute | solution.py:114
  155.0 31.1 %collective-permute-start.2 = (f32[2048,160]{0,1:T(8,128)S(1)}, f32[2048,160]{0,1:T(8,128)S(1)}, u32[]{:S(2)}, u32[]{:S(2)}) collective-permute-start(f32[2048,160]{0,1:T(8,128)S(1)} %add.139), channel_id=1, source_target_pairs={{0,2},{1,3},{2,0},{3,1},{4,6},{5,7},{6,4},{7,5},{8,10},{9,11},{10,... | collective-permute-start | bytes 3932168 | tf_op jit(solution)/shard_map/ppermute | solution.py:114
  186.3 36.5 %copy-start.11 = (bf16[256]{0:T(256)(128)(2,1)S(1)}, bf16[256]{0:T(256)(128)(2,1)}, u32[]{:S(2)}) copy-start(bf16[256]{0:T(256)(128)(2,1)} %param.28) | copy-start | bytes 1540
  186.3 36.5 %copy-start.12 = (s32[8]{0:T(128)S(1)}, s32[8]{0:T(128)}, u32[]{:S(2)}) copy-start(s32[8]{0:T(128)} %param.20) | copy-start | bytes 100
  186.3 28.7 %collective-permute-start.3 = (f32[2048,160]{0,1:T(8,128)S(1)}, f32[2048,160]{0,1:T(8,128)S(1)}, u32[]{:S(2)}, u32[]{:S(2)}) collective-permute-start(f32[2048,160]{0,1:T(8,128)S(1)} %add.140), channel_id=1, source_target_pairs={{0,4},{1,5},{2,6},{3,7},{4,0},{5,1},{6,2},{7,3},{8,12},{9,13},{10,... | collective-permute-start | bytes 3932168 | tf_op jit(solution)/shard_map/ppermute | solution.py:114
  215.2 40.1 %collective-permute-start.4 = (f32[2048,160]{0,1:T(8,128)S(1)}, f32[2048,160]{0,1:T(8,128)}, u32[]{:S(2)}, u32[]{:S(2)}) collective-permute-start(f32[2048,160]{0,1:T(8,128)S(1)} %add.141), channel_id=1, source_target_pairs={{0,8},{1,9},{2,10},{3,11},{4,12},{5,13},{6,14},{7,15},{8,0},{9,1},... | collective-permute-start | bytes 3932168 | tf_op jit(solution)/shard_map/ppermute | solution.py:114
  218.2 41.4 %all-to-all-start.1 = ((bf16[16,128,256]{2,1,0:T(8,128)(2,1)}), bf16[16,128,256]{2,1,0:T(8,128)(2,1)S(1)}, u32[]{:S(2)}, u32[]{:S(2)}) async-start(bf16[16,128,256]{2,1,0:T(8,128)(2,1)} %bitcast.17), calls=%async_computation.1 | async-start | bytes 2097152 | tf_op jit(solution)/shard_map/all_to_all | solution.py:125
  222.8 33.9 %copy-start.9 = (bf16[128,256]{1,0:T(8,128)(2,1)S(1)}, bf16[128,256]{1,0:T(8,128)(2,1)}, u32[]{:S(2)}) copy-start(bf16[128,256]{1,0:T(8,128)(2,1)} %param.27) | copy-start | bytes 196612
  256.7 1.5 copy-start.5
  258.2 7.5 %copy-start.7 = (f32[4096]{0:T(1024)S(1)}, f32[4096]{0:T(1024)}, u32[]{:S(2)}) copy-start(f32[4096]{0:T(1024)} %param.30) | copy-start | bytes 49156
  259.6 19.2 %all-to-all-start = ((bf16[16,128,256]{1,2,0:T(8,128)(2,1)}), bf16[16,128,256]{1,2,0:T(8,128)(2,1)S(1)}, u32[]{:S(2)}, u32[]{:S(2)}) async-start(bf16[16,128,256]{1,2,0:T(8,128)(2,1)} %copy.43), calls=%async_computation | async-start | bytes 2097152 | tf_op jit(solution)/shard_map/all_to_all | solution.py:126
  264.9 310.5 %all-gather.9.cloned.1.call-start = ((), (), s32[]{:S(2)}) async-start(), calls=%async_computation.6 | async-start | bytes 1179648 | tf_op jit(solution)/shard_map/all_gather | solution.py:124
  286.3 1.8 copy-start.6
  286.7 1.4 copy-start.3
  345.0 8.4 %collective-permute-start = (f32[16,4096]{1,0:T(8,128)S(1)}, f32[16,4096]{1,0:T(8,128)S(1)}, u32[]{:S(2)}, u32[]{:S(2)}) collective-permute-start(f32[16,4096]{1,0:T(8,128)S(1)} %bitcast_add_fusion.3), channel_id=1, source_target_pairs={{0,1},{1,2},{2,3},{3,4},{4,5},{5,6},{6,7},{7,8},{8,9},{9,10},{10,1... | collective-permute-start | bytes 786440 | tf_op jit(solution)/shard_map/while/body/eval_jaxpr/ppermute | solution.py:13
  353.4 10.7 %collective-permute-start = (f32[16,4096]{1,0:T(8,128)S(1)}, f32[16,4096]{1,0:T(8,128)S(1)}, u32[]{:S(2)}, u32[]{:S(2)}) collective-permute-start(f32[16,4096]{1,0:T(8,128)S(1)} %bitcast_add_fusion.3), channel_id=1, source_target_pairs={{0,1},{1,2},{2,3},{3,4},{4,5},{5,6},{6,7},{7,8},{8,9},{9,10},{10,1... | collective-permute-start | bytes 786440 | tf_op jit(solution)/shard_map/while/body/eval_jaxpr/ppermute | solution.py:13
  364.1 9.8 %collective-permute-start = (f32[16,4096]{1,0:T(8,128)S(1)}, f32[16,4096]{1,0:T(8,128)S(1)}, u32[]{:S(2)}, u32[]{:S(2)}) collective-permute-start(f32[16,4096]{1,0:T(8,128)S(1)} %bitcast_add_fusion.3), channel_id=1, source_target_pairs={{0,1},{1,2},{2,3},{3,4},{4,5},{5,6},{6,7},{7,8},{8,9},{9,10},{10,1... | collective-permute-start | bytes 786440 | tf_op jit(solution)/shard_map/while/body/eval_jaxpr/ppermute | solution.py:13
  373.9 8.9 %collective-permute-start = (f32[16,4096]{1,0:T(8,128)S(1)}, f32[16,4096]{1,0:T(8,128)S(1)}, u32[]{:S(2)}, u32[]{:S(2)}) collective-permute-start(f32[16,4096]{1,0:T(8,128)S(1)} %bitcast_add_fusion.3), channel_id=1, source_target_pairs={{0,1},{1,2},{2,3},{3,4},{4,5},{5,6},{6,7},{7,8},{8,9},{9,10},{10,1... | collective-permute-start | bytes 786440 | tf_op jit(solution)/shard_map/while/body/eval_jaxpr/ppermute | solution.py:13
  382.9 8.3 %collective-permute-start = (f32[16,4096]{1,0:T(8,128)S(1)}, f32[16,4096]{1,0:T(8,128)S(1)}, u32[]{:S(2)}, u32[]{:S(2)}) collective-permute-start(f32[16,4096]{1,0:T(8,128)S(1)} %bitcast_add_fusion.3), channel_id=1, source_target_pairs={{0,1},{1,2},{2,3},{3,4},{4,5},{5,6},{6,7},{7,8},{8,9},{9,10},{10,1... | collective-permute-start | bytes 786440 | tf_op jit(solution)/shard_map/while/body/eval_jaxpr/ppermute | solution.py:13
  391.2 10.0 %collective-permute-start = (f32[16,4096]{1,0:T(8,128)S(1)}, f32[16,4096]{1,0:T(8,128)S(1)}, u32[]{:S(2)}, u32[]{:S(2)}) collective-permute-start(f32[16,4096]{1,0:T(8,128)S(1)} %bitcast_add_fusion.3), channel_id=1, source_target_pairs={{0,1},{1,2},{2,3},{3,4},{4,5},{5,6},{6,7},{7,8},{8,9},{9,10},{10,1... | collective-permute-start | bytes 786440 | tf_op jit(solution)/shard_map/while/body/eval_jaxpr/ppermute | solution.py:13
  401.2 9.5 %collective-permute-start = (f32[16,4096]{1,0:T(8,128)S(1)}, f32[16,4096]{1,0:T(8,128)S(1)}, u32[]{:S(2)}, u32[]{:S(2)}) collective-permute-start(f32[16,4096]{1,0:T(8,128)S(1)} %bitcast_add_fusion.3), channel_id=1, source_target_pairs={{0,1},{1,2},{2,3},{3,4},{4,5},{5,6},{6,7},{7,8},{8,9},{9,10},{10,1... | collective-permute-start | bytes 786440 | tf_op jit(solution)/shard_map/while/body/eval_jaxpr/ppermute | solution.py:13
  410.8 10.4 %collective-permute-start = (f32[16,4096]{1,0:T(8,128)S(1)}, f32[16,4096]{1,0:T(8,128)S(1)}, u32[]{:S(2)}, u32[]{:S(2)}) collective-permute-start(f32[16,4096]{1,0:T(8,128)S(1)} %bitcast_add_fusion.3), channel_id=1, source_target_pairs={{0,1},{1,2},{2,3},{3,4},{4,5},{5,6},{6,7},{7,8},{8,9},{9,10},{10,1... | collective-permute-start | bytes 786440 | tf_op jit(solution)/shard_map/while/body/eval_jaxpr/ppermute | solution.py:13
  421.2 10.4 %collective-permute-start = (f32[16,4096]{1,0:T(8,128)S(1)}, f32[16,4096]{1,0:T(8,128)S(1)}, u32[]{:S(2)}, u32[]{:S(2)}) collective-permute-start(f32[16,4096]{1,0:T(8,128)S(1)} %bitcast_add_fusion.3), channel_id=1, source_target_pairs={{0,1},{1,2},{2,3},{3,4},{4,5},{5,6},{6,7},{7,8},{8,9},{9,10},{10,1... | collective-permute-start | bytes 786440 | tf_op jit(solution)/shard_map/while/body/eval_jaxpr/ppermute | solution.py:13
  431.6 10.4 %collective-permute-start = (f32[16,4096]{1,0:T(8,128)S(1)}, f32[16,4096]{1,0:T(8,128)S(1)}, u32[]{:S(2)}, u32[]{:S(2)}) collective-permute-start(f32[16,4096]{1,0:T(8,128)S(1)} %bitcast_add_fusion.3), channel_id=1, source_target_pairs={{0,1},{1,2},{2,3},{3,4},{4,5},{5,6},{6,7},{7,8},{8,9},{9,10},{10,1... | collective-permute-start | bytes 786440 | tf_op jit(solution)/shard_map/while/body/eval_jaxpr/ppermute | solution.py:13
  442.0 10.6 %collective-permute-start = (f32[16,4096]{1,0:T(8,128)S(1)}, f32[16,4096]{1,0:T(8,128)S(1)}, u32[]{:S(2)}, u32[]{:S(2)}) collective-permute-start(f32[16,4096]{1,0:T(8,128)S(1)} %bitcast_add_fusion.3), channel_id=1, source_target_pairs={{0,1},{1,2},{2,3},{3,4},{4,5},{5,6},{6,7},{7,8},{8,9},{9,10},{10,1... | collective-permute-start | bytes 786440 | tf_op jit(solution)/shard_map/while/body/eval_jaxpr/ppermute | solution.py:13
  452.7 12.0 %collective-permute-start = (f32[16,4096]{1,0:T(8,128)S(1)}, f32[16,4096]{1,0:T(8,128)S(1)}, u32[]{:S(2)}, u32[]{:S(2)}) collective-permute-start(f32[16,4096]{1,0:T(8,128)S(1)} %bitcast_add_fusion.3), channel_id=1, source_target_pairs={{0,1},{1,2},{2,3},{3,4},{4,5},{5,6},{6,7},{7,8},{8,9},{9,10},{10,1... | collective-permute-start | bytes 786440 | tf_op jit(solution)/shard_map/while/body/eval_jaxpr/ppermute | solution.py:13
  464.8 13.5 %collective-permute-start = (f32[16,4096]{1,0:T(8,128)S(1)}, f32[16,4096]{1,0:T(8,128)S(1)}, u32[]{:S(2)}, u32[]{:S(2)}) collective-permute-start(f32[16,4096]{1,0:T(8,128)S(1)} %bitcast_add_fusion.3), channel_id=1, source_target_pairs={{0,1},{1,2},{2,3},{3,4},{4,5},{5,6},{6,7},{7,8},{8,9},{9,10},{10,1... | collective-permute-start | bytes 786440 | tf_op jit(solution)/shard_map/while/body/eval_jaxpr/ppermute | solution.py:13
  478.3 11.3 %collective-permute-start = (f32[16,4096]{1,0:T(8,128)S(1)}, f32[16,4096]{1,0:T(8,128)S(1)}, u32[]{:S(2)}, u32[]{:S(2)}) collective-permute-start(f32[16,4096]{1,0:T(8,128)S(1)} %bitcast_add_fusion.3), channel_id=1, source_target_pairs={{0,1},{1,2},{2,3},{3,4},{4,5},{5,6},{6,7},{7,8},{8,9},{9,10},{10,1... | collective-permute-start | bytes 786440 | tf_op jit(solution)/shard_map/while/body/eval_jaxpr/ppermute | solution.py:13
  489.6 10.4 %collective-permute-start = (f32[16,4096]{1,0:T(8,128)S(1)}, f32[16,4096]{1,0:T(8,128)S(1)}, u32[]{:S(2)}, u32[]{:S(2)}) collective-permute-start(f32[16,4096]{1,0:T(8,128)S(1)} %bitcast_add_fusion.3), channel_id=1, source_target_pairs={{0,1},{1,2},{2,3},{3,4},{4,5},{5,6},{6,7},{7,8},{8,9},{9,10},{10,1... | collective-permute-start | bytes 786440 | tf_op jit(solution)/shard_map/while/body/eval_jaxpr/ppermute | solution.py:13
  542.8 30.3 %all-to-all-start.2 = ((bf16[128,16,256]{2,0,1:T(8,128)(2,1)}), bf16[128,16,256]{2,0,1:T(8,128)(2,1)S(1)}, u32[]{:S(2)}, u32[]{:S(2)}) async-start(bf16[128,16,256]{2,0,1:T(8,128)(2,1)} %fusion.30), calls=%async_computation.2 | async-start | bytes 2097152 | tf_op jit(solution)/shard_map/all_to_all | solution.py:149
  559.8 89.0 %all-reduce.3.cloned.1.call-start = ((), (), s32[]{:S(2)}) async-start(), calls=%async_computation.8 | async-start | bytes 262144 | tf_op jit(solution)/shard_map/psum | solution.py:18
  560.6 176.9 %reduce-scatter.2.cloned.1.call-start = ((), (), s32[]{:S(2)}) async-start(), calls=%async_computation.7 | async-start | bytes 8912896 | tf_op jit(solution)/shard_map/reduce_scatter | solution.py:153
  582.3 0.7 copy-start.13
  582.3 155.3 %copy-start.2 = (bf16[1,128,2048]{2,1,0:T(8,128)(2,1)S(1)}, bf16[1,128,2048]{2,1,0:T(8,128)(2,1)}, u32[]{:S(2)}) copy-start(bf16[1,128,2048]{2,1,0:T(8,128)(2,1)} %param.19) | copy-start | bytes 1572868
  582.3 157.2 %copy-start.1 = (bf16[256,160]{0,1:T(8,128)(2,1)S(1)}, bf16[256,160]{0,1:T(8,128)(2,1)}, u32[]{:S(2)}) copy-start(bf16[256,160]{0,1:T(8,128)(2,1)} %param.26) | copy-start | bytes 245764
Sparse Core Ops, SparseCore 0:
  9.7 27.7 all-gather.6
  40.2 71.2 all-gather.4
  267.4 24.7 all-gather.8
  564.0 84.6 all-reduce.2
  652.0 85.4 reduce-scatter.1
